TPU v7x, 256 devices: a whole 4x4x8 slice. The times are simulated.
256 devices in a mesh: expert: 16 (over x, y), dp: 16 (over z, core).
Axes of the slice: x: 4, y: 4, z: 8, core: 2. Of those that a mesh axis runs over, the one named last changes fastest.
Arguments:
- tokens: bfloat16 [4096, 4096], P(('expert', 'dp')), may hold values from -6 to 6
- grad_out: bfloat16 [4096, 4096], P(('expert', 'dp')), may hold values from -6 to 6
- gate_values: bfloat16 [4096, 2], P(('expert', 'dp')), may hold values from 0.099609375 to 1
- routes: int32 [4096, 2], P(('expert', 'dp')), may hold values from 0 to 31, all different within a row; in each aligned block of 16 rows (0 to 15, 16 to 31, ...) at most 2 rows name the same one
- gate_weight: bfloat16 [32, 1536, 4096], P('expert', 'dp'), may hold values from -0.09375 to 0.09375
- up_weight: bfloat16 [32, 1536, 4096], P('expert', 'dp'), may hold values from -0.09375 to 0.09375
- down_weight: bfloat16 [32, 1536, 4096], P('expert', 'dp'), may hold values from -0.15625 to 0.15625
Outputs:
- grad_tokens: bfloat16 [4096, 4096], P(('expert', 'dp'))
- grad_gates: float32 [4096, 2], P(('expert', 'dp'))
- grad_gate_weight: bfloat16 [32, 1536, 4096], P('expert', 'dp')
- grad_up_weight: bfloat16 [32, 1536, 4096], P('expert', 'dp')
- grad_down_weight: bfloat16 [32, 1536, 4096], P('expert', 'dp')
Inputs may be any that keep to these rules, and one draw needn't show every extreme that they name: `routes`: each row names 2 different experts. In each aligned block of 16 rows (the rows of one device) no expert is named by more than 2 rows, a bound that some block reaches.
All inputs are finite; a program needn't handle non-finite values.
Results may differ from a plain program's by a relative error of at most 0.019.
Values may be sent and summed in bfloat16 or wider, within the bound.
No kernel may reach another device: no remote copies, remote signals or barrier semaphores. Data moves between devices by JAX's collectives and lax.ppermute only.
A program may use at most 128 MiB of HBM per device.

v0:
```python
import jax
import jax.numpy as jnp
from jax import lax
from jax.sharding import PartitionSpec as P

PAD = 128


def per_device(tokens, grad_out, gate_values, routes, gate_weight, up_weight, down_weight):
    f32, bf16 = (jnp.float32, jnp.bfloat16)
    tok_rows, model_width = tokens.shape
    chosen = routes.shape[1]
    local_experts = gate_weight.shape[0]
    groups = lax.axis_size("expert")
    n_dp = lax.axis_size("dp")
    experts_all = local_experts * groups
    capacity = 2 * tok_rows * chosen // experts_all
    slot_count = experts_all * capacity
    block_rows = groups * capacity
    gathered_rows = n_dp * block_rows
    width = 2 * model_width + PAD
    back_width = model_width + PAD
    flat_routes = routes.reshape(-1)
    onehot = (flat_routes[:, None] == jnp.arange(experts_all, dtype=jnp.int32)[None, :]).astype(
        jnp.int32
    )
    earlier = jnp.cumsum(onehot, axis=0) - onehot
    slot_rank = jnp.sum(earlier * onehot, axis=1)
    owner_col = flat_routes // local_experts
    local_id = flat_routes % local_experts
    slot_index = (local_id * groups + owner_col) * capacity + slot_rank
    placing = (jnp.arange(slot_count, dtype=jnp.int32)[:, None] == slot_index[None, :]).astype(f32)
    token_map = jnp.sum(placing.reshape(slot_count, tok_rows, chosen), axis=2).astype(bf16)
    slot_gates = jnp.dot(
        placing.astype(bf16), gate_values.reshape(-1), preferred_element_type=f32
    ).astype(bf16)
    x_slots = jnp.dot(token_map, tokens, preferred_element_type=f32).astype(bf16)
    dy_slots = jnp.dot(token_map, grad_out, preferred_element_type=f32).astype(bf16)
    gate_cols = jnp.concatenate(
        [slot_gates[:, None], jnp.zeros((slot_count, PAD - 1), bf16)], axis=1
    )
    payload = jnp.concatenate([x_slots, dy_slots, gate_cols], axis=1)
    payload = payload.reshape(local_experts, groups, capacity, width)
    extra_rows = (
        jnp.arange(back_width, dtype=jnp.int32)[None, :]
        == model_width + jnp.arange(2, dtype=jnp.int32)[:, None]
    ).astype(bf16)
    backs, ggw, guw, gdw = ([], [], [], [])
    for l in range(local_experts):
        with jax.named_scope(f"expert_{l}"):
            blk = lax.all_to_all(payload[l], "expert", split_axis=0, concat_axis=0, tiled=True)
            blk = blk.reshape(block_rows, width)
            rows = lax.all_gather(blk, "dp", axis=0).reshape(gathered_rows, width)
            inputs = rows[:, :model_width]
            upstream = rows[:, model_width : 2 * model_width]
            weighting = rows[:, 2 * model_width].astype(f32)[:, None]
            gw, uw, dw = (gate_weight[l], up_weight[l], down_weight[l])
            gate_pre = jnp.einsum("rd,hd->rh", inputs, gw, preferred_element_type=f32)
            up_pre = jnp.einsum("rd,hd->rh", inputs, uw, preferred_element_type=f32)
            back_hidden = jnp.einsum("rd,hd->rh", upstream, dw, preferred_element_type=f32)
            sigmoid_gate = jax.nn.sigmoid(gate_pre)
            activated = gate_pre * sigmoid_gate
            hidden = activated * up_pre
            gate_part = jnp.sum(back_hidden * hidden, axis=1)
            scaled = weighting * back_hidden
            grad_gate_pre = (
                scaled * up_pre * sigmoid_gate * (1.0 + gate_pre * (1.0 - sigmoid_gate))
            ).astype(bf16)
            grad_up_pre = (scaled * activated).astype(bf16)
            weighted_hidden = (weighting * hidden).astype(bf16)
            hi = gate_part.astype(bf16)
            lo = (gate_part - hi.astype(f32)).astype(bf16)
            lhs = jnp.concatenate([grad_gate_pre, grad_up_pre, hi[:, None], lo[:, None]], axis=1)
            stacked = jnp.pad(jnp.concatenate([gw, uw], axis=0), ((0, 0), (0, PAD)))
            rhs = jnp.concatenate([stacked, extra_rows], axis=0)
            back = jnp.dot(lhs, rhs, preferred_element_type=f32).astype(bf16)
            backs.append(back.reshape(n_dp, block_rows, back_width))
            ggw.append(
                jnp.einsum("rh,rd->hd", grad_gate_pre, inputs, preferred_element_type=f32).astype(
                    bf16
                )
            )
            guw.append(
                jnp.einsum("rh,rd->hd", grad_up_pre, inputs, preferred_element_type=f32).astype(
                    bf16
                )
            )
            gdw.append(
                jnp.einsum(
                    "rh,rd->hd", weighted_hidden, upstream, preferred_element_type=f32
                ).astype(bf16)
            )
    back = lax.psum_scatter(jnp.concatenate(backs, axis=1), "dp", scatter_dimension=0, tiled=True)
    back = back.reshape(local_experts, groups, capacity, back_width)
    returned = lax.all_to_all(back, "expert", split_axis=1, concat_axis=1, tiled=True)
    returned = returned.reshape(slot_count, back_width)
    grad_tokens = lax.dot_general(
        token_map, returned[:, :model_width], (((0,), (0,)), ((), ())), preferred_element_type=f32
    ).astype(bf16)
    gate_back = returned[:, model_width].astype(f32) + returned[:, model_width + 1].astype(f32)
    grad_gates = jnp.dot(gate_back, placing, precision=lax.Precision.HIGHEST).reshape(
        tok_rows, chosen
    )
    return (grad_tokens, grad_gates, jnp.stack(ggw), jnp.stack(guw), jnp.stack(gdw))


def solution(mesh):
    rows = P(("expert", "dp"), None)
    blocks = P("expert", "dp", None)
    return jax.shard_map(
        per_device,
        mesh=mesh,
        in_specs=(rows, rows, rows, rows, blocks, blocks, blocks),
        out_specs=(rows, rows, blocks, blocks, blocks),
        check_vma=False,
    )
```

profile of v0, /device:TPU:8, one launch (start us, length us, event | category | flops | bytes accessed | tf_op | source)
XLA Modules:
  0.0 272.8 jit_solution(8301096907189134309)
XLA Ops:
  12.5 17.7 %all_to_all.15 = bf16[16,2,8320]{2,1,0:T(2,128)(2,1)S(1)} all-to-all(bf16[16,2,8320]{2,1,0:T(2,128)(2,1)S(1)} %squeeze.28), channel_id=1, replica_groups=mesh['expert'=16,'dp'=16] {'expert'}, dimensions={0} | all-to-all | bytes 1064960 | tf_op jit(solution)/shard_map/expert_0/all_to_all | solution.py:51
  31.4 14.0 %all_to_all.16 = bf16[16,2,8320]{2,1,0:T(2,128)(2,1)S(1)} all-to-all(bf16[16,2,8320]{2,1,0:T(2,128)(2,1)S(1)} %squeeze.32), channel_id=1, replica_groups=mesh['expert'=16,'dp'=16] {'expert'}, dimensions={0} | all-to-all | bytes 1064960 | tf_op jit(solution)/shard_map/expert_1/all_to_all | solution.py:51
  46.6 1.5 slice_bitcast_fusion.2
  48.6 39.4 %all-gather.3.cloned.1.call-done = bf16[16,32,8320]{2,1,0:T(8,128)(2,1)} async-done(((bf16[1,32,8320]{2,1,0:T(8,128)(2,1)}), bf16[16,32,8320]{2,1,0:T(8,128)(2,1)}) %all-gather.3.cloned.1.call-update) | async-done | bytes 8519696 | tf_op jit(solution)/shard_map/expert_0/all_gather | solution.py:53
  89.0 4.5 %fusion.26 = f32[512,96]{0,1:T(8,128)} fusion(bf16[512,8320]{1,0:T(8,128)(2,1)} %bitcast.78, bf16[2,96,4096]{2,1,0:T(8,128)(2,1)} %param.12), kind=kOutput, calls=%fused_computation.39 | convolution fusion | flops 402653184 | bytes 5177344 | tf_op jit(solution)/shard_map/expert_0/rd,hd->rh/dot_general | solution.py:59
  93.5 51.9 %all-gather.5.cloned.1.call-done = bf16[16,32,8320]{2,1,0:T(8,128)(2,1)} async-done(((bf16[1,32,8320]{2,1,0:T(8,128)(2,1)}), bf16[16,32,8320]{2,1,0:T(8,128)(2,1)}) %all-gather.5.cloned.1.call-update) | async-done | bytes 8519696 | tf_op jit(solution)/shard_map/expert_1/all_gather | solution.py:53
  145.4 4.0 %fusion.20 = f32[512,96]{0,1:T(8,128)S(1)} fusion(bf16[512,8320]{1,0:T(8,128)(2,1)} %bitcast.70, bf16[2,96,4096]{2,1,0:T(8,128)(2,1)} %param.12), kind=kOutput, calls=%fused_computation.33 | convolution fusion | flops 402653184 | bytes 5177344 | tf_op jit(solution)/shard_map/expert_1/rd,hd->rh/dot_general | solution.py:59
  149.4 1.5 convert_reduce_fusion
  150.9 4.0 %fusion.10 = f32[512,96]{0,1:T(8,128)S(1)} fusion(bf16[512,8320]{1,0:T(8,128)(2,1)} %bitcast.79, bf16[2,96,4096]{2,1,0:T(8,128)(2,1)} %param.13), kind=kOutput, calls=%fused_computation.22 | convolution fusion | flops 402653184 | bytes 5177344 | tf_op jit(solution)/shard_map/expert_0/rd,hd->rh/dot_general | solution.py:60
  156.5 2.1 multiply_convert_fusion.5
  158.6 2.1 multiply_convert_fusion.3
  160.7 3.4 %convolution_convert_fusion.1 = bf16[512,4224]{1,0:T(8,128)(2,1)} fusion(bf16[2,4224]{1,0:T(2,128)(2,1)S(1)} %compare_convert_fusion, bf16[192,4224]{1,0:T(8,128)(2,1)S(1)} %get-tuple-element.19, bf16[512,1]{0,1:T(2,128)(2,1)S(1)} %subtract_convert_fusion.1, bf16[512,1]{0,1:T(2,128)(2,1)S(1)} %convert_element_type.167, ...), kind=kOutput, calls=%fused_computation.2 | convolution fusion | flops 845358080 | bytes 6162944 | tf_op jit(solution)/shard_map/expert_0/dot_general | solution.py:76
  164.1 3.5 %convolution_convert_fusion = bf16[512,4224]{1,0:T(8,128)(2,1)} fusion(bf16[2,4224]{1,0:T(2,128)(2,1)S(1)} %compare_convert_fusion, bf16[192,4224]{1,0:T(8,128)(2,1)S(1)} %get-tuple-element.20, bf16[512,1]{0,1:T(2,128)(2,1)S(1)} %subtract_convert_fusion, bf16[512,1]{0,1:T(2,128)(2,1)S(1)} %convert_element_type.174, ...), kind=kOutput, calls=%fused_computation.1 | convolution fusion | flops 845358080 | bytes 6162944 | tf_op jit(solution)/shard_map/expert_1/dot_general | solution.py:76
  167.6 7.8 %pad_maximum_fusion = bf16[16,64,4224]{2,1,0:T(8,128)(2,1)} fusion(bf16[16,32,4224]{2,1,0:T(8,128)(2,1)} %bitcast.65, bf16[16,32,4224]{2,1,0:T(8,128)(2,1)} %bitcast.64), kind=kLoop, calls=%fused_computation | loop fusion | flops 17301504 | bytes 17301504 | tf_op jit(solution)/shard_map/concatenate | solution.py:93
  176.3 3.0 %fusion = bf16[1,96,4096]{2,1,0:T(8,128)(2,1)S(1)} fusion(bf16[512,96]{0,1:T(8,128)(2,1)S(1)} %copy-done.7, bf16[512,8320]{1,0:T(8,128)(2,1)} %bitcast.80), kind=kOutput, calls=%fused_computation.9 | convolution fusion | flops 403046400 | bytes 5079040 | tf_op jit(solution)/shard_map/expert_0/rh,rd->hd/dot_general | solution.py:79
  179.3 3.0 %fusion.2 = bf16[1,96,4096]{2,1,0:T(8,128)(2,1)S(1)} fusion(bf16[512,96]{0,1:T(8,128)(2,1)S(1)} %get-tuple-element.15, bf16[512,8320]{1,0:T(8,128)(2,1)} %bitcast.81), kind=kOutput, calls=%fused_computation.11 | convolution fusion | flops 403046400 | bytes 5079040 | tf_op jit(solution)/shard_map/expert_0/rh,rd->hd/dot_general | solution.py:84
  182.4 3.0 %fusion.1 = bf16[1,96,4096]{2,1,0:T(8,128)(2,1)S(1)} fusion(bf16[512,96]{0,1:T(8,128)(2,1)S(1)} %copy-done.11, bf16[512,8320]{1,0:T(8,128)(2,1)} %bitcast.72), kind=kOutput, calls=%fused_computation.10 | convolution fusion | flops 403046400 | bytes 5079040 | tf_op jit(solution)/shard_map/expert_1/rh,rd->hd/dot_general | solution.py:79
  185.4 3.1 %fusion.3 = bf16[1,96,4096]{2,1,0:T(8,128)(2,1)S(1)} fusion(bf16[512,96]{0,1:T(8,128)(2,1)S(1)} %copy-done.9, bf16[512,8320]{1,0:T(8,128)(2,1)} %bitcast.73), kind=kOutput, calls=%fused_computation.12 | convolution fusion | flops 403046400 | bytes 5079040 | tf_op jit(solution)/shard_map/expert_1/rh,rd->hd/dot_general | solution.py:84
  188.5 3.2 %fusion.4 = bf16[1,96,4096]{2,1,0:T(8,128)(2,1)S(1)} fusion(bf16[512,8320]{1,0:T(8,128)(2,1)} %bitcast.82, f32[512]{0:T(512)S(1)} %convert_reduce_fusion.1, f32[512,96]{0,1:T(8,128)S(1)} %copy-done.16, f32[512,96]{0,1:T(8,128)S(1)} %copy-done.17), kind=kOutput, calls=%fused_computation.13 | convolution fusion | flops 403390464 | bytes 5376000 | tf_op jit(solution)/shard_map/expert_0/rh,rd->hd/dot_general | solution.py:89
  191.8 1.9 pad_maximum_fusion.5
  193.7 51.7 %reduce-scatter.2.cloned.1.call-done = bf16[1,64,4224]{2,1,0:T(8,128)(2,1)} async-done(((bf16[16,64,4224]{2,1,0:T(8,128)(2,1)}), bf16[1,64,4224]{2,1,0:T(8,128)(2,1)}) %reduce-scatter.2.cloned.1.call-update) | async-done | bytes 540688 | tf_op jit(solution)/shard_map/reduce_scatter | solution.py:93
  247.8 7.3 %all-to-all-start.2 = ((bf16[2,16,2,4224]{3,2,0,1:T(2,128)(2,1)}), bf16[2,16,2,4224]{3,2,0,1:T(2,128)(2,1)S(1)}, u32[]{:S(2)}, u32[]{:S(2)}) async-start(bf16[2,16,2,4224]{3,2,0,1:T(2,128)(2,1)} %copy.61), calls=%async_computation.3 | async-start | bytes 1081344 | tf_op jit(solution)/shard_map/all_to_all | solution.py:95
  255.1 3.0 %fusion.5 = bf16[1,96,4096]{2,1,0:T(8,128)(2,1)S(1)} fusion(bf16[512,8320]{1,0:T(8,128)(2,1)} %bitcast.74, f32[512]{0:T(512)S(1)} %convert_reduce_fusion, f32[512,96]{0,1:T(8,128)S(1)} %copy-done.13, f32[512,96]{0,1:T(8,128)S(1)} %copy-done.14), kind=kOutput, calls=%fused_computation.14 | convolution fusion | flops 403390464 | bytes 5376000 | tf_op jit(solution)/shard_map/expert_1/rh,rd->hd/dot_general | solution.py:89
  259.4 4.5 %all-to-all-done.2 = bf16[2,16,2,4224]{3,2,0,1:T(2,128)(2,1)S(1)} async-done(((bf16[2,16,2,4224]{3,2,0,1:T(2,128)(2,1)}), bf16[2,16,2,4224]{3,2,0,1:T(2,128)(2,1)S(1)}, u32[]{:S(2)}, u32[]{:S(2)}) %all-to-all-start.2) | async-done | bytes 540704 | tf_op jit(solution)/shard_map/all_to_all | solution.py:95
  (85 shorter events, 17.8 us)
Async XLA Ops:
  7.2 2.6 copy-start
  7.2 80.8 %all-gather.3.cloned.1.call-start = ((), (), s32[]{:S(2)}) async-start(), calls=%async_computation.4 | async-start | bytes 9052160 | tf_op jit(solution)/shard_map/expert_0/all_gather | solution.py:53
  31.1 114.3 %all-gather.5.cloned.1.call-start = ((), (), s32[]{:S(2)}) async-start(), calls=%async_computation.5 | async-start | bytes 9052160 | tf_op jit(solution)/shard_map/expert_1/all_gather | solution.py:53
  31.2 16.9 %copy-start.1 = (bf16[2,96,4096]{2,1,0:T(8,128)(2,1)S(1)}, bf16[2,96,4096]{2,1,0:T(8,128)(2,1)}, u32[]{:S(2)}) copy-start(bf16[2,96,4096]{2,1,0:T(8,128)(2,1)} %param.12) | copy-start | bytes 4718596
  46.4 199.0 %reduce-scatter.2.cloned.1.call-start = ((), (), s32[]{:S(2)}) async-start(), calls=%async_computation.6 | async-start | bytes 9191424 | tf_op jit(solution)/shard_map/reduce_scatter | solution.py:93
  145.4 9.4 %copy-start.3 = (bf16[16,32,8320]{2,1,0:T(8,128)(2,1)S(1)}, bf16[16,32,8320]{2,1,0:T(8,128)(2,1)}, u32[]{:S(2)}) copy-start(bf16[16,32,8320]{2,1,0:T(8,128)(2,1)} %all-gather.5.cloned.1.call-done) | copy-start | bytes 25559044
  145.4 9.5 %copy-start.5 = (bf16[2,96,4096]{2,1,0:T(8,128)(2,1)S(1)}, bf16[2,96,4096]{2,1,0:T(8,128)(2,1)}, u32[]{:S(2)}) copy-start(bf16[2,96,4096]{2,1,0:T(8,128)(2,1)} %param.13) | copy-start | bytes 4718596
  149.4 9.2 %copy-start.12 = (f32[512,96]{0,1:T(8,128)}, f32[512,96]{0,1:T(8,128)S(1)}, u32[]{:S(2)}) copy-start(f32[512,96]{0,1:T(8,128)S(1)} %fusion.20) | copy-start | bytes 589828
  150.8 5.4 %copy-start.4 = (bf16[16,32,8320]{2,1,0:T(8,128)(2,1)S(1)}, bf16[16,32,8320]{2,1,0:T(8,128)(2,1)}, u32[]{:S(2)}) copy-start(bf16[16,32,8320]{2,1,0:T(8,128)(2,1)} %all-gather.3.cloned.1.call-done) | copy-start | bytes 25559044
  154.8 1.6 copy-start.2
  154.9 1.6 copy-start.15
  158.6 2.1 copy-start.6
  160.7 6.9 %copy-start.8 = (bf16[512,96]{0,1:T(8,128)(2,1)}, bf16[512,96]{0,1:T(8,128)(2,1)S(1)}, u32[]{:S(2)}) copy-start(bf16[512,96]{0,1:T(8,128)(2,1)S(1)} %get-tuple-element.16) | copy-start | bytes 294916
  160.7 6.9 %copy-start.10 = (bf16[512,96]{0,1:T(8,128)(2,1)}, bf16[512,96]{0,1:T(8,128)(2,1)S(1)}, u32[]{:S(2)}) copy-start(bf16[512,96]{0,1:T(8,128)(2,1)S(1)} %get-tuple-element.13) | copy-start | bytes 294916
  175.4 0.9 copy-start.7
  179.3 3.1 %copy-start.11 = (bf16[512,96]{0,1:T(8,128)(2,1)S(1)}, bf16[512,96]{0,1:T(8,128)(2,1)}, u32[]{:S(2)}) copy-start(bf16[512,96]{0,1:T(8,128)(2,1)} %copy-done.10) | copy-start | bytes 294916
  182.3 3.0 %copy-start.9 = (bf16[512,96]{0,1:T(8,128)(2,1)S(1)}, bf16[512,96]{0,1:T(8,128)(2,1)}, u32[]{:S(2)}) copy-start(bf16[512,96]{0,1:T(8,128)(2,1)} %copy-done.8) | copy-start | bytes 294916
  185.4 3.1 %copy-start.16 = (f32[512,96]{0,1:T(8,128)S(1)}, f32[512,96]{0,1:T(8,128)}, u32[]{:S(2)}) copy-start(f32[512,96]{0,1:T(8,128)} %fusion.26) | copy-start | bytes 589828
  185.4 3.1 %copy-start.17 = (f32[512,96]{0,1:T(8,128)S(1)}, f32[512,96]{0,1:T(8,128)}, u32[]{:S(2)}) copy-start(f32[512,96]{0,1:T(8,128)} %get-tuple-element.18) | copy-start | bytes 589828
  191.7 63.3 %copy-start.13 = (f32[512,96]{0,1:T(8,128)S(1)}, f32[512,96]{0,1:T(8,128)}, u32[]{:S(2)}) copy-start(f32[512,96]{0,1:T(8,128)} %copy-done.12) | copy-start | bytes 589828
  191.7 63.3 %copy-start.14 = (f32[512,96]{0,1:T(8,128)S(1)}, f32[512,96]{0,1:T(8,128)}, u32[]{:S(2)}) copy-start(f32[512,96]{0,1:T(8,128)} %get-tuple-element.17) | copy-start | bytes 589828
  247.8 16.1 %all-to-all-start.2 = ((bf16[2,16,2,4224]{3,2,0,1:T(2,128)(2,1)}), bf16[2,16,2,4224]{3,2,0,1:T(2,128)(2,1)S(1)}, u32[]{:S(2)}, u32[]{:S(2)}) async-start(bf16[2,16,2,4224]{3,2,0,1:T(2,128)(2,1)} %copy.61), calls=%async_computation.3 | async-start | bytes 1081344 | tf_op jit(solution)/shard_map/all_to_all | solution.py:95
Sparse Core Ops, SparseCore 0:
  31.3 56.6 all-gather.2
  90.3 55.0 all-gather.4
  175.5 69.8 reduce-scatter.1
where the time goes:
time: 273 us
  waiting for transfers between devices  148 us (54%)
  matrix products  46.5 us (17%)
  blocking collectives  31.6 us (12%)
  other arithmetic  14.5 us (5%)
  between operations  14.1 us (5%)
  local copies, waits for them, and re-layouts  10.9 us (4%)
  starting transfers between devices  7.56 us (3%)
    all_gather x2, waiting for transfers between devices, per_device(): rows = lax.all_gather(blk, 'dp', axis=0).reshape(gathered_rows, width)  91.3 us
    reduce_scatter x1, waiting for transfers between devices, per_device(): lax.psum_scatter(jnp.concatenate(backs, axis=1), 'dp', scatter_dimension=...  51.7 us
    all_to_all x2, blocking collectives, per_device(): lax.all_to_all(payload[l], 'expert', split_axis=0, concat_axis=0, tiled=T...  31.6 us
    dot_general x2, matrix products, per_device(): up_pre = jnp.einsum('rd,hd->rh', inputs, uw, preferred_element_type=f32)  8.46 us
    concatenate x1, other arithmetic, per_device(): jnp.concatenate(backs, axis=1)  7.8 us
    all_to_all x1, starting transfers between devices, per_device(): lax.all_to_all(back, 'expert', split_axis=1, concat_axis=1, tiled=True)  7.26 us
    dot_general x2, matrix products, per_device(): back = jnp.dot(lhs, rhs, preferred_element_type=f32).astype(bf16)  6.85 us
    dot_general x2, matrix products, per_device(): jnp.einsum('rh,rd->hd', weighted_hidden, upstream, preferred_element_type...  6.2 us
  transfers between devices with their start and end apart: 4, of which 4 were waited for; matrix products, arithmetic and copies ran while one was open for 11% of the time, Pallas kernels for 0%

commit v1 on v0

--- a/solution.py
+++ b/solution.py
@@ -4,6 +4,12 @@
 from jax.sharding import PartitionSpec as P
 
 PAD = 128
+
+
+def trade_parts(x, axis, split, join):
+    cells = jnp.split(x, lax.axis_size(axis), axis=split)
+    arrived = lax.all_to_all(jnp.stack(cells), axis, 0, 0)
+    return jnp.concatenate(arrived, axis=join)
 
 
 def per_device(tokens, grad_out, gate_values, routes, gate_weight, up_weight, down_weight):
@@ -92,7 +98,7 @@
             )
     back = lax.psum_scatter(jnp.concatenate(backs, axis=1), "dp", scatter_dimension=0, tiled=True)
     back = back.reshape(local_experts, groups, capacity, back_width)
-    returned = lax.all_to_all(back, "expert", split_axis=1, concat_axis=1, tiled=True)
+    returned = trade_parts(back, "expert", 1, 1)
     returned = returned.reshape(slot_count, back_width)
     grad_tokens = lax.dot_general(
         token_map, returned[:, :model_width], (((0,), (0,)), ((), ())), preferred_element_type=f32

time: 273 us -> 282 us (1.033)
  local copies, waits for them, and re-layouts: 10.9 us -> 19.9 us
    unnamed x38 -> x53, local copies, waits for them, and re-layouts: 2.62 us -> 12.1 us
where the time goes in v1:
time: 282 us
  waiting for transfers between devices  148 us (52%)
  matrix products  46.4 us (16%)
  blocking collectives  31.6 us (11%)
  local copies, waits for them, and re-layouts  19.9 us (7%)
  other arithmetic  14.5 us (5%)
  between operations  14.2 us (5%)
  starting transfers between devices  7.56 us (3%)
    all_gather x2, waiting for transfers between devices, per_device(): rows = lax.all_gather(blk, 'dp', axis=0).reshape(gathered_rows, width)  91.3 us
    reduce_scatter x1, waiting for transfers between devices, per_device(): lax.psum_scatter(jnp.concatenate(backs, axis=1), 'dp', scatter_dimension=...  51.7 us
    all_to_all x2, blocking collectives, per_device(): lax.all_to_all(payload[l], 'expert', split_axis=0, concat_axis=0, tiled=T...  31.6 us
    unnamed x53, local copies, waits for them, and re-layouts  12.1 us
    dot_general x2, matrix products, per_device(): up_pre = jnp.einsum('rd,hd->rh', inputs, uw, preferred_element_type=f32)  8.46 us
    concatenate x1, other arithmetic, per_device(): jnp.concatenate(backs, axis=1)  7.8 us
    all_to_all x1, starting transfers between devices, trade_parts(): arrived = lax.all_to_all(jnp.stack(cells), axis, 0, 0)  7.26 us
    dot_general x2, matrix products, per_device(): back = jnp.dot(lhs, rhs, preferred_element_type=f32).astype(bf16)  6.85 us
  transfers between devices with their start and end apart: 4, of which 4 were waited for; matrix products, arithmetic and copies ran while one was open for 11% of the time, Pallas kernels for 0%

profile of v1, /device:TPU:8, one launch (start us, length us, event | category | flops | bytes accessed | tf_op | source)
XLA Modules:
  0.0 281.8 jit_solution(5443694744459264933)
XLA Ops:
  12.5 17.7 %all_to_all.15 = bf16[16,2,8320]{2,1,0:T(2,128)(2,1)S(1)} all-to-all(bf16[16,2,8320]{2,1,0:T(2,128)(2,1)S(1)} %squeeze.28), channel_id=1, replica_groups=mesh['expert'=16,'dp'=16] {'expert'}, dimensions={0} | all-to-all | bytes 1064960 | tf_op jit(solution)/shard_map/expert_0/all_to_all | solution.py:57
  31.4 14.0 %all_to_all.16 = bf16[16,2,8320]{2,1,0:T(2,128)(2,1)S(1)} all-to-all(bf16[16,2,8320]{2,1,0:T(2,128)(2,1)S(1)} %squeeze.32), channel_id=1, replica_groups=mesh['expert'=16,'dp'=16] {'expert'}, dimensions={0} | all-to-all | bytes 1064960 | tf_op jit(solution)/shard_map/expert_1/all_to_all | solution.py:57
  46.6 1.5 slice_bitcast_fusion.2
  48.6 39.4 %all-gather.3.cloned.1.call-done = bf16[16,32,8320]{2,1,0:T(8,128)(2,1)} async-done(((bf16[1,32,8320]{2,1,0:T(8,128)(2,1)}), bf16[16,32,8320]{2,1,0:T(8,128)(2,1)}) %all-gather.3.cloned.1.call-update) | async-done | bytes 8519696 | tf_op jit(solution)/shard_map/expert_0/all_gather | solution.py:59
  89.0 4.5 %fusion.26 = f32[512,96]{0,1:T(8,128)} fusion(bf16[512,8320]{1,0:T(8,128)(2,1)} %bitcast.146, bf16[2,96,4096]{2,1,0:T(8,128)(2,1)} %param.12), kind=kOutput, calls=%fused_computation.39 | convolution fusion | flops 402653184 | bytes 5177344 | tf_op jit(solution)/shard_map/expert_0/rd,hd->rh/dot_general | solution.py:65
  93.5 51.9 %all-gather.5.cloned.1.call-done = bf16[16,32,8320]{2,1,0:T(8,128)(2,1)} async-done(((bf16[1,32,8320]{2,1,0:T(8,128)(2,1)}), bf16[16,32,8320]{2,1,0:T(8,128)(2,1)}) %all-gather.5.cloned.1.call-update) | async-done | bytes 8519696 | tf_op jit(solution)/shard_map/expert_1/all_gather | solution.py:59
  145.4 4.0 %fusion.20 = f32[512,96]{0,1:T(8,128)S(1)} fusion(bf16[512,8320]{1,0:T(8,128)(2,1)} %bitcast.138, bf16[2,96,4096]{2,1,0:T(8,128)(2,1)} %param.12), kind=kOutput, calls=%fused_computation.33 | convolution fusion | flops 402653184 | bytes 5177344 | tf_op jit(solution)/shard_map/expert_1/rd,hd->rh/dot_general | solution.py:65
  149.4 1.5 convert_reduce_fusion
  150.9 4.0 %fusion.10 = f32[512,96]{0,1:T(8,128)S(1)} fusion(bf16[512,8320]{1,0:T(8,128)(2,1)} %bitcast.147, bf16[2,96,4096]{2,1,0:T(8,128)(2,1)} %param.13), kind=kOutput, calls=%fused_computation.22 | convolution fusion | flops 402653184 | bytes 5177344 | tf_op jit(solution)/shard_map/expert_0/rd,hd->rh/dot_general | solution.py:66
  156.5 2.1 multiply_convert_fusion.5
  158.6 2.1 multiply_convert_fusion.3
  160.7 3.4 %convolution_convert_fusion.1 = bf16[512,4224]{1,0:T(8,128)(2,1)} fusion(bf16[2,4224]{1,0:T(2,128)(2,1)S(1)} %compare_convert_fusion, bf16[192,4224]{1,0:T(8,128)(2,1)S(1)} %get-tuple-element.19, bf16[512,1]{0,1:T(2,128)(2,1)S(1)} %subtract_convert_fusion.1, bf16[512,1]{0,1:T(2,128)(2,1)S(1)} %convert_element_type.167, ...), kind=kOutput, calls=%fused_computation.2 | convolution fusion | flops 845358080 | bytes 6162944 | tf_op jit(solution)/shard_map/expert_0/dot_general | solution.py:82
  164.1 3.5 %convolution_convert_fusion = bf16[512,4224]{1,0:T(8,128)(2,1)} fusion(bf16[2,4224]{1,0:T(2,128)(2,1)S(1)} %compare_convert_fusion, bf16[192,4224]{1,0:T(8,128)(2,1)S(1)} %get-tuple-element.20, bf16[512,1]{0,1:T(2,128)(2,1)S(1)} %subtract_convert_fusion, bf16[512,1]{0,1:T(2,128)(2,1)S(1)} %convert_element_type.174, ...), kind=kOutput, calls=%fused_computation.1 | convolution fusion | flops 845358080 | bytes 6162944 | tf_op jit(solution)/shard_map/expert_1/dot_general | solution.py:82
  167.6 7.8 %pad_maximum_fusion = bf16[16,64,4224]{2,1,0:T(8,128)(2,1)} fusion(bf16[16,32,4224]{2,1,0:T(8,128)(2,1)} %bitcast.132, bf16[16,32,4224]{2,1,0:T(8,128)(2,1)} %bitcast.131), kind=kLoop, calls=%fused_computation | loop fusion | flops 17301504 | bytes 17301504 | tf_op jit(solution)/shard_map/concatenate | solution.py:99
  176.3 3.0 %fusion = bf16[1,96,4096]{2,1,0:T(8,128)(2,1)S(1)} fusion(bf16[512,96]{0,1:T(8,128)(2,1)S(1)} %copy-done.7, bf16[512,8320]{1,0:T(8,128)(2,1)} %bitcast.148), kind=kOutput, calls=%fused_computation.9 | convolution fusion | flops 403046400 | bytes 5079040 | tf_op jit(solution)/shard_map/expert_0/rh,rd->hd/dot_general | solution.py:85
  179.3 3.0 %fusion.2 = bf16[1,96,4096]{2,1,0:T(8,128)(2,1)S(1)} fusion(bf16[512,96]{0,1:T(8,128)(2,1)S(1)} %get-tuple-element.15, bf16[512,8320]{1,0:T(8,128)(2,1)} %bitcast.149), kind=kOutput, calls=%fused_computation.11 | convolution fusion | flops 403046400 | bytes 5079040 | tf_op jit(solution)/shard_map/expert_0/rh,rd->hd/dot_general | solution.py:90
  182.4 3.0 %fusion.1 = bf16[1,96,4096]{2,1,0:T(8,128)(2,1)S(1)} fusion(bf16[512,96]{0,1:T(8,128)(2,1)S(1)} %copy-done.11, bf16[512,8320]{1,0:T(8,128)(2,1)} %bitcast.140), kind=kOutput, calls=%fused_computation.10 | convolution fusion | flops 403046400 | bytes 5079040 | tf_op jit(solution)/shard_map/expert_1/rh,rd->hd/dot_general | solution.py:85
  185.4 3.1 %fusion.3 = bf16[1,96,4096]{2,1,0:T(8,128)(2,1)S(1)} fusion(bf16[512,96]{0,1:T(8,128)(2,1)S(1)} %copy-done.9, bf16[512,8320]{1,0:T(8,128)(2,1)} %bitcast.141), kind=kOutput, calls=%fused_computation.12 | convolution fusion | flops 403046400 | bytes 5079040 | tf_op jit(solution)/shard_map/expert_1/rh,rd->hd/dot_general | solution.py:90
  188.5 3.2 %fusion.4 = bf16[1,96,4096]{2,1,0:T(8,128)(2,1)S(1)} fusion(bf16[512,8320]{1,0:T(8,128)(2,1)} %bitcast.150, f32[512]{0:T(512)S(1)} %convert_reduce_fusion.1, f32[512,96]{0,1:T(8,128)S(1)} %copy-done.16, f32[512,96]{0,1:T(8,128)S(1)} %copy-done.17), kind=kOutput, calls=%fused_computation.13 | convolution fusion | flops 403390464 | bytes 5376000 | tf_op jit(solution)/shard_map/expert_0/rh,rd->hd/dot_general | solution.py:95
  191.8 1.9 pad_maximum_fusion.5
  193.7 51.7 %reduce-scatter.2.cloned.1.call-done = bf16[1,64,4224]{2,1,0:T(8,128)(2,1)} async-done(((bf16[16,64,4224]{2,1,0:T(8,128)(2,1)}), bf16[1,64,4224]{2,1,0:T(8,128)(2,1)}) %reduce-scatter.2.cloned.1.call-update) | async-done | bytes 540688 | tf_op jit(solution)/shard_map/reduce_scatter | solution.py:99
  256.8 7.3 %all-to-all-start.2 = ((bf16[16,2,1,2,4224]{4,3,1,2,0:T(2,128)(2,1)}), bf16[16,2,1,2,4224]{4,3,1,2,0:T(2,128)(2,1)S(1)}, u32[]{:S(2)}, u32[]{:S(2)}) async-start(bf16[16,2,1,2,4224]{4,3,1,2,0:T(2,128)(2,1)} %constant_dynamic-update-slice_fusion), calls=%async_computation.3 | async-start | bytes 1081344 | tf_op jit(solution)/shard_map/all_to_all | solution.py:11
  264.0 3.0 %fusion.5 = bf16[1,96,4096]{2,1,0:T(8,128)(2,1)S(1)} fusion(bf16[512,8320]{1,0:T(8,128)(2,1)} %bitcast.142, f32[512]{0:T(512)S(1)} %convert_reduce_fusion, f32[512,96]{0,1:T(8,128)S(1)} %copy-done.13, f32[512,96]{0,1:T(8,128)S(1)} %copy-done.14), kind=kOutput, calls=%fused_computation.14 | convolution fusion | flops 403390464 | bytes 5376000 | tf_op jit(solution)/shard_map/expert_1/rh,rd->hd/dot_general | solution.py:95
  268.3 4.5 %all-to-all-done.2 = bf16[16,2,1,2,4224]{4,3,1,2,0:T(2,128)(2,1)S(1)} async-done(((bf16[16,2,1,2,4224]{4,3,1,2,0:T(2,128)(2,1)}), bf16[16,2,1,2,4224]{4,3,1,2,0:T(2,128)(2,1)S(1)}, u32[]{:S(2)}, u32[]{:S(2)}) %all-to-all-start.2) | async-done | bytes 540704 | tf_op jit(solution)/shard_map/all_to_all | solution.py:11
  (100 shorter events, 26.7 us)
Async XLA Ops:
  7.2 2.6 copy-start
  7.2 80.8 %all-gather.3.cloned.1.call-start = ((), (), s32[]{:S(2)}) async-start(), calls=%async_computation.4 | async-start | bytes 9052160 | tf_op jit(solution)/shard_map/expert_0/all_gather | solution.py:59
  31.1 114.3 %all-gather.5.cloned.1.call-start = ((), (), s32[]{:S(2)}) async-start(), calls=%async_computation.5 | async-start | bytes 9052160 | tf_op jit(solution)/shard_map/expert_1/all_gather | solution.py:59
  31.2 16.9 %copy-start.1 = (bf16[2,96,4096]{2,1,0:T(8,128)(2,1)S(1)}, bf16[2,96,4096]{2,1,0:T(8,128)(2,1)}, u32[]{:S(2)}) copy-start(bf16[2,96,4096]{2,1,0:T(8,128)(2,1)} %param.12) | copy-start | bytes 4718596
  46.4 199.0 %reduce-scatter.2.cloned.1.call-start = ((), (), s32[]{:S(2)}) async-start(), calls=%async_computation.6 | async-start | bytes 9191424 | tf_op jit(solution)/shard_map/reduce_scatter | solution.py:99
  145.4 9.4 %copy-start.3 = (bf16[16,32,8320]{2,1,0:T(8,128)(2,1)S(1)}, bf16[16,32,8320]{2,1,0:T(8,128)(2,1)}, u32[]{:S(2)}) copy-start(bf16[16,32,8320]{2,1,0:T(8,128)(2,1)} %all-gather.5.cloned.1.call-done) | copy-start | bytes 25559044
  145.4 9.5 %copy-start.5 = (bf16[2,96,4096]{2,1,0:T(8,128)(2,1)S(1)}, bf16[2,96,4096]{2,1,0:T(8,128)(2,1)}, u32[]{:S(2)}) copy-start(bf16[2,96,4096]{2,1,0:T(8,128)(2,1)} %param.13) | copy-start | bytes 4718596
  149.4 9.2 %copy-start.12 = (f32[512,96]{0,1:T(8,128)}, f32[512,96]{0,1:T(8,128)S(1)}, u32[]{:S(2)}) copy-start(f32[512,96]{0,1:T(8,128)S(1)} %fusion.20) | copy-start | bytes 589828
  150.8 5.4 %copy-start.4 = (bf16[16,32,8320]{2,1,0:T(8,128)(2,1)S(1)}, bf16[16,32,8320]{2,1,0:T(8,128)(2,1)}, u32[]{:S(2)}) copy-start(bf16[16,32,8320]{2,1,0:T(8,128)(2,1)} %all-gather.3.cloned.1.call-done) | copy-start | bytes 25559044
  154.8 1.6 copy-start.2
  154.9 1.6 copy-start.15
  158.6 2.1 copy-start.6
  160.7 6.9 %copy-start.8 = (bf16[512,96]{0,1:T(8,128)(2,1)}, bf16[512,96]{0,1:T(8,128)(2,1)S(1)}, u32[]{:S(2)}) copy-start(bf16[512,96]{0,1:T(8,128)(2,1)S(1)} %get-tuple-element.16) | copy-start | bytes 294916
  160.7 6.9 %copy-start.10 = (bf16[512,96]{0,1:T(8,128)(2,1)}, bf16[512,96]{0,1:T(8,128)(2,1)S(1)}, u32[]{:S(2)}) copy-start(bf16[512,96]{0,1:T(8,128)(2,1)S(1)} %get-tuple-element.13) | copy-start | bytes 294916
  175.4 0.9 copy-start.7
  179.3 3.1 %copy-start.11 = (bf16[512,96]{0,1:T(8,128)(2,1)S(1)}, bf16[512,96]{0,1:T(8,128)(2,1)}, u32[]{:S(2)}) copy-start(bf16[512,96]{0,1:T(8,128)(2,1)} %copy-done.10) | copy-start | bytes 294916
  182.3 3.0 %copy-start.9 = (bf16[512,96]{0,1:T(8,128)(2,1)S(1)}, bf16[512,96]{0,1:T(8,128)(2,1)}, u32[]{:S(2)}) copy-start(bf16[512,96]{0,1:T(8,128)(2,1)} %copy-done.8) | copy-start | bytes 294916
  185.4 3.1 %copy-start.16 = (f32[512,96]{0,1:T(8,128)S(1)}, f32[512,96]{0,1:T(8,128)}, u32[]{:S(2)}) copy-start(f32[512,96]{0,1:T(8,128)} %fusion.26) | copy-start | bytes 589828
  185.4 3.1 %copy-start.17 = (f32[512,96]{0,1:T(8,128)S(1)}, f32[512,96]{0,1:T(8,128)}, u32[]{:S(2)}) copy-start(f32[512,96]{0,1:T(8,128)} %get-tuple-element.18) | copy-start | bytes 589828
  191.7 72.3 %copy-start.13 = (f32[512,96]{0,1:T(8,128)S(1)}, f32[512,96]{0,1:T(8,128)}, u32[]{:S(2)}) copy-start(f32[512,96]{0,1:T(8,128)} %copy-done.12) | copy-start | bytes 589828
  191.7 72.3 %copy-start.14 = (f32[512,96]{0,1:T(8,128)S(1)}, f32[512,96]{0,1:T(8,128)}, u32[]{:S(2)}) copy-start(f32[512,96]{0,1:T(8,128)} %get-tuple-element.17) | copy-start | bytes 589828
  256.8 16.1 %all-to-all-start.2 = ((bf16[16,2,1,2,4224]{4,3,1,2,0:T(2,128)(2,1)}), bf16[16,2,1,2,4224]{4,3,1,2,0:T(2,128)(2,1)S(1)}, u32[]{:S(2)}, u32[]{:S(2)}) async-start(bf16[16,2,1,2,4224]{4,3,1,2,0:T(2,128)(2,1)} %constant_dynamic-update-slice_fusion), calls=%async_computation.3 | async-start | bytes 1081344 | tf_op jit(solution)/shard_map/all_to_all | solution.py:11
Sparse Core Ops, SparseCore 0:
  31.3 56.6 all-gather.2
  90.3 55.0 all-gather.4
  175.5 69.8 reduce-scatter.1
